TPU v7x, 32 devices: a whole 2x2x4 slice. The times are simulated.
32 devices in a mesh: req: 8 (over z, y), ep: 4 (over x, core).
Axes of the slice: x: 2, y: 2, z: 4, core: 2. Of those that a mesh axis runs over, the one named last changes fastest.
Arguments:
- tokens: bfloat16 [4096, 1536], P(('req', 'ep')), may hold values from -6 to 6
- seg_ids: int32 [4096], P(('req', 'ep')), may hold values from 0 to 3, never falling along the last dimension, each value on 1 to 2048 neighbouring positions
- routes: int32 [4096, 8], P(('req', 'ep')), may hold values from 0 to 39, all different within a row; in each aligned block of 128 rows (0 to 127, 128 to 255, ...) at most 48 rows name the same one
- route_weights: float32 [4096, 8], P(('req', 'ep')), may hold values from 0.05 to 0.3
- norm1_gain: float32 [1536], replicated, may hold values from 0.5 to 1.5
- norm2_gain: float32 [1536], replicated, may hold values from 0.5 to 1.5
- w_query: bfloat16 [1536, 1536], P(None, 'ep')
- key_weight: bfloat16 [1536, 512], P(None, 'ep')
- value_weight: bfloat16 [1536, 512], P(None, 'ep'), may hold values from -0.15625 to 0.15625
- w_out_attn: bfloat16 [1536, 1536], P('ep'), may hold values from -0.15625 to 0.15625
- w_in: bfloat16 [40, 1536, 1024], P('ep'), may hold values from -0.15625 to 0.15625
- w_out: bfloat16 [40, 512, 1536], P('ep'), may hold values from -0.25 to 0.25
- paged_key_value_cache: bfloat16 [96, 8, 2, 64, 64], P('req', 'ep'), may hold values from -6 to 6
- page_table: int32 [64], replicated, may hold values from 0 to 95, as said below
Outputs:
- attn_out: bfloat16 [4096, 1536], P(('req', 'ep'))
- moe_out: bfloat16 [4096, 1536], P(('req', 'ep'))
- new_cache: bfloat16 [96, 8, 2, 64, 64], P('req', 'ep')
Inputs may be any that keep to these rules, and one draw needn't show every extreme that they name: `seg_ids`: segment ids never fall along the stream; the longest prompt holds exactly half of the 4096 tokens. `routes`: each token names 8 different experts; within the rows of one device no expert is named more than 48 times, a bound that some block reaches. `page_table`: entries are distinct.
All inputs are finite; a program needn't handle non-finite values.
Results may differ from a plain program's by a relative error of at most 0.017.
Values may be sent and summed in bfloat16 or wider, within the bound.
No kernel may reach another device: no remote copies, remote signals or barrier semaphores. Data moves between devices by JAX's collectives and lax.ppermute only.
A program may use at most 192 MiB of HBM per device.

v0:
```python
import jax
import jax.numpy as jnp
from jax import lax
from jax.sharding import PartitionSpec as P
from jax.experimental import pallas as pl
from jax.experimental.pallas import tpu as pltpu

HEAD_SIZE = 64
E = 40
PAGE_TOKENS = 64
CAP = 48


norm_eps = 1e-06
score_scale = 0.015625
residual_scale = 0.22
rope_base = 10000.0
neg_fill = -1e30


def rms_scale(rows, gain):
    mean_sq = jnp.mean(rows * rows, axis=-1, keepdims=True)
    return rows * lax.rsqrt(mean_sq + norm_eps) * gain


def positions_of(segments):
    tok_index = jnp.arange(segments.shape[0], dtype=jnp.int32)
    previous = jnp.concatenate([jnp.full((1,), -1, jnp.int32), segments[:-1]])
    starts = jnp.where(segments != previous, tok_index, 0)
    return tok_index - lax.cummax(starts, axis=0)


def rotary_apply(heads_in, token_positions):
    half_dim = heads_in.shape[-1] // 2
    inverse_freq = rope_base ** (
        -jnp.arange(half_dim, dtype=jnp.float32) * 2.0 / heads_in.shape[-1]
    )
    angles = token_positions.astype(jnp.float32)[:, None] * inverse_freq[None, :]
    cos_part = jnp.cos(angles)[:, None, :]
    sine_part = jnp.sin(angles)[:, None, :]
    first_half = heads_in[..., :half_dim]
    second_half = heads_in[..., half_dim:]
    return jnp.concatenate(
        [
            first_half * cos_part - second_half * sine_part,
            second_half * cos_part + first_half * sine_part,
        ],
        axis=-1,
    )


def gather_rows(x, axis_name, axis=0):
    count = lax.axis_size(axis_name)
    spread = jnp.broadcast_to(x[None], (count,) + x.shape)
    got = lax.all_to_all(spread, axis_name, 0, 0, tiled=True)
    got = jnp.moveaxis(got, 0, axis)
    shape = list(x.shape)
    shape[axis] = shape[axis] * count
    return got.reshape(shape)


def scatter_sum_rows(x, axis_name):
    count = lax.axis_size(axis_name)
    parts = x.reshape((count, x.shape[0] // count) + x.shape[1:])
    got = lax.all_to_all(parts, axis_name, 0, 0, tiled=True)
    return jnp.sum(got.astype(jnp.float32), axis=0)


def chip_pairs(count, shift):
    chips = count // 2
    return [(d, ((d // 2 + shift) % chips) * 2 + d % 2) for d in range(count)]


def gather_ep(x):
    count = lax.axis_size("ep")
    if count % 2:
        return gather_rows(x, "ep")
    chips = count // 2
    me = lax.axis_index("ep")
    chip = me // 2
    core = me % 2
    side = [x]
    for shift in range(1, chips):
        side.append(lax.ppermute(x, "ep", chip_pairs(count, shift)))
    side = jnp.stack(side)
    other = lax.ppermute(side, "ep", [(d, d ^ 1) for d in range(count)])
    both = jnp.where(core == 0, jnp.stack([side, other], 1), jnp.stack([other, side], 1))
    order = (chip - jnp.arange(chips, dtype=jnp.int32)) % chips
    full = jnp.take(both, order, axis=0, mode="clip")
    return full.reshape((count * x.shape[0],) + x.shape[1:])


def scatter_sum_ep(p):
    count = lax.axis_size("ep")
    if count % 2:
        return scatter_sum_rows(p, "ep")
    chips = count // 2
    me = lax.axis_index("ep")
    chip = me // 2
    core = me % 2
    rows = p.shape[0] // count
    parts = p.reshape((chips, 2, rows) + p.shape[1:])
    mine = jnp.where(core == 0, parts[:, 0], parts[:, 1])
    theirs = jnp.where(core == 0, parts[:, 1], parts[:, 0])
    got = lax.ppermute(theirs, "ep", [(d, d ^ 1) for d in range(count)])
    sums = mine.astype(jnp.float32) + got.astype(jnp.float32)
    total = lax.dynamic_index_in_dim(sums, chip, 0, keepdims=False)
    for shift in range(1, chips):
        piece = lax.dynamic_index_in_dim(sums, (chip + shift) % chips, 0, keepdims=False)
        total = total + lax.ppermute(
            piece.astype(jnp.bfloat16), "ep", chip_pairs(count, shift)
        ).astype(jnp.float32)
    return total


Q_TILE = 256
K_TILE = 512


def flash_body(lo_ref, hi_ref, q_ref, k_ref, v_ref, tok_ref, begin_ref, o_ref):
    qb = pl.program_id(1)
    ratio = q_ref.shape[1]
    q_tile = q_ref.shape[2]
    head_dim = q_ref.shape[3]
    q = q_ref[0].reshape(ratio * q_tile, head_dim)
    per_group = k_ref.shape[2] // K_TILE
    tok = tok_ref[...]
    begin = begin_ref[...]

    def step(kb, carry):
        m_old, l_old, acc_old = carry
        k0 = kb * K_TILE
        grp = kb // per_group
        off = pl.multiple_of((kb % per_group) * K_TILE, K_TILE)
        k_blk = k_ref[grp, 0, pl.ds(off, K_TILE), :]
        v_blk = v_ref[grp, 0, pl.ds(off, K_TILE), :]
        s = lax.dot_general(
            q, k_blk, (((1,), (1,)), ((), ())), preferred_element_type=jnp.float32
        )
        s = (s * score_scale).reshape(ratio, q_tile, K_TILE)
        key_at = k0 + lax.broadcasted_iota(jnp.int32, (q_tile, K_TILE), 1)
        allowed = (key_at >= begin) & (key_at <= tok)
        s = jnp.where(allowed[None], s, -jnp.inf)
        m_new = jnp.maximum(m_old, jnp.max(s, axis=-1, keepdims=True))
        alpha = jnp.exp(m_old - m_new)
        p = jnp.exp(s - m_new)
        l_new = alpha * l_old + jnp.sum(p, axis=-1, keepdims=True)
        pv = lax.dot_general(
            p.reshape(ratio * q_tile, K_TILE).astype(jnp.bfloat16),
            v_blk,
            (((1,), (0,)), ((), ())),
            preferred_element_type=jnp.float32,
        )
        acc_new = alpha * acc_old + pv.reshape(ratio, q_tile, head_dim)
        return m_new, l_new, acc_new

    init = (
        jnp.full((ratio, q_tile, 1), neg_fill, jnp.float32),
        jnp.zeros((ratio, q_tile, 1), jnp.float32),
        jnp.zeros((ratio, q_tile, head_dim), jnp.float32),
    )
    m_fin, l_fin, acc_fin = lax.fori_loop(lo_ref[qb], hi_ref[qb] + 1, step, init)
    o_ref[0] = (acc_fin / l_fin).astype(o_ref.dtype)


def flash_attention(query_grouped, kv_all, q_index, q_begin):
    kv_heads, ratio, group_len, head_dim = query_grouped.shape
    n_grp, _, grp_len, _ = kv_all.shape
    n_q = group_len // Q_TILE
    lo = jnp.min(q_begin.reshape(n_q, Q_TILE), axis=1) // K_TILE
    hi = jnp.max(q_index.reshape(n_q, Q_TILE), axis=1) // K_TILE
    grid_spec = pltpu.PrefetchScalarGridSpec(
        num_scalar_prefetch=2,
        grid=(kv_heads, n_q),
        in_specs=[
            pl.BlockSpec((1, ratio, Q_TILE, head_dim), lambda g, qb, lo, hi: (g, 0, qb, 0)),
            pl.BlockSpec((n_grp, 1, grp_len, head_dim), lambda g, qb, lo, hi: (0, g, 0, 0)),
            pl.BlockSpec(
                (n_grp, 1, grp_len, head_dim), lambda g, qb, lo, hi: (0, kv_heads + g, 0, 0)
            ),
            pl.BlockSpec((Q_TILE, 1), lambda g, qb, lo, hi: (qb, 0)),
            pl.BlockSpec((Q_TILE, 1), lambda g, qb, lo, hi: (qb, 0)),
        ],
        out_specs=pl.BlockSpec((1, ratio, Q_TILE, head_dim), lambda g, qb, lo, hi: (g, 0, qb, 0)),
    )
    out = pl.pallas_call(
        flash_body,
        grid_spec=grid_spec,
        out_shape=jax.ShapeDtypeStruct(query_grouped.shape, jnp.bfloat16),
    )(lo, hi, query_grouped, kv_all, kv_all, q_index[:, None], q_begin[:, None])
    return out


def body(
    tokens,
    seg_ids,
    routes,
    route_weights,
    norm1_gain,
    norm2_gain,
    w_query,
    key_weight,
    value_weight,
    w_out_attn,
    w_in,
    w_out,
    paged_key_value_cache,
    page_table,
):
    tok_dev = tokens.shape[0]
    ep_count = lax.axis_size("ep")
    group_len = tok_dev * ep_count
    req_pos = lax.axis_index("req")
    normed = rms_scale(tokens.astype(jnp.float32), norm1_gain).astype(jnp.bfloat16)
    seg_ids, normed = lax.optimization_barrier((seg_ids, normed))
    all_segs = gather_rows(seg_ids, ("req", "ep"))
    all_pos = positions_of(all_segs)
    group_start = req_pos * group_len
    group_pos = lax.dynamic_slice_in_dim(all_pos, group_start, group_len)
    joined = jnp.concatenate([w_query, key_weight, value_weight], axis=1)
    projected = jnp.dot(
        gather_ep(normed), joined, preferred_element_type=jnp.float32
    )
    query_width = w_query.shape[1]
    kv_width = key_weight.shape[1]
    q_heads = query_width // HEAD_SIZE
    kv_heads = kv_width // HEAD_SIZE
    heads_ratio = q_heads // kv_heads
    query_rows = rotary_apply(
        projected[:, :query_width].reshape(group_len, q_heads, HEAD_SIZE), group_pos
    ).astype(jnp.bfloat16)
    key_rows = rotary_apply(
        projected[:, query_width : query_width + kv_width].reshape(
            group_len, kv_heads, HEAD_SIZE
        ),
        group_pos,
    ).astype(jnp.bfloat16)
    value_rows = (
        projected[:, query_width + kv_width :]
        .astype(jnp.bfloat16)
        .reshape(group_len, kv_heads, HEAD_SIZE)
    )
    query_grouped = query_rows.reshape(group_len, kv_heads, heads_ratio, HEAD_SIZE).transpose(
        1, 2, 0, 3
    )
    kv_local = jnp.concatenate(
        [key_rows.transpose(1, 0, 2), value_rows.transpose(1, 0, 2)], axis=0
    )
    req_count = lax.axis_size("req")
    kv_all = lax.all_to_all(
        jnp.broadcast_to(kv_local[None], (req_count,) + kv_local.shape), "req", 0, 0, tiled=True
    )
    q_index = group_start + jnp.arange(group_len, dtype=jnp.int32)
    q_begin = q_index - group_pos
    head_out = flash_attention(query_grouped, kv_all, q_index, q_begin)
    pages_here = paged_key_value_cache.shape[0]
    page_first = req_pos * pages_here
    group_pages = group_len // PAGE_TOKENS
    local_pages = page_first + jnp.arange(pages_here, dtype=jnp.int32)
    match = local_pages[:, None] == page_table[None, :]
    hit = jnp.any(match, axis=1)
    block_of = jnp.argmax(match, axis=1).astype(jnp.int32)
    kv_paged = kv_all.reshape(req_count, 2, kv_heads, group_pages, PAGE_TOKENS, HEAD_SIZE)
    picked = kv_paged[block_of // group_pages, :, :, block_of % group_pages].transpose(
        0, 2, 1, 3, 4
    )
    new_cache = jnp.where(hit[:, None, None, None, None], picked, paged_key_value_cache)
    out_weight = w_out_attn.reshape(kv_heads, heads_ratio, HEAD_SIZE, w_out_attn.shape[1])
    attention = scatter_sum_ep(
        jnp.einsum(
            "grtd,grdo->to", head_out, out_weight, preferred_element_type=jnp.float32
        ).astype(jnp.bfloat16)
    )
    attn_out = attention.astype(jnp.bfloat16)
    moe_in = rms_scale(tokens.astype(jnp.float32) + residual_scale * attention, norm2_gain).astype(
        jnp.bfloat16
    )
    ffe_width = w_out.shape[1]
    exp_here = w_in.shape[0]
    expert_ids = jnp.arange(E, dtype=jnp.int32)
    shares = jnp.sum(
        jnp.where(routes[:, :, None] == expert_ids[None, None, :], route_weights[:, :, None], 0.0),
        axis=1,
    )
    rows_all = gather_ep(moe_in)
    shares_all = gather_rows(shares, "ep")
    first_expert = lax.axis_index("ep") * exp_here
    shares_here = lax.dynamic_slice_in_dim(shares_all, first_expert, exp_here, 1)
    total_rows = rows_all.shape[0]
    chosen = (shares_here > 0.0).astype(jnp.int32).reshape(ep_count, tok_dev, exp_here)
    slot_in = jnp.cumsum(chosen, axis=1) - 1
    source_ids = jnp.arange(ep_count, dtype=jnp.int32)[:, None, None]
    local_slot = (source_ids * CAP + slot_in).reshape(total_rows, exp_here)
    live = (chosen > 0).reshape(total_rows, exp_here)
    slot_ids = jnp.arange(ep_count * CAP, dtype=jnp.int32)
    dispatch = (local_slot.T[:, None, :] == slot_ids[None, :, None]) & live.T[:, None, :]
    arrived = jnp.einsum(
        "esr,rd->esd", dispatch.astype(jnp.bfloat16), rows_all, preferred_element_type=jnp.float32
    ).astype(jnp.bfloat16)
    gate_up = jnp.einsum("esd,edf->esf", arrived, w_in, preferred_element_type=jnp.float32)
    activated = (jax.nn.silu(gate_up[..., :ffe_width]) * gate_up[..., ffe_width:]).astype(
        jnp.bfloat16
    )
    result = jnp.einsum(
        "esf,efd->esd", activated, w_out, preferred_element_type=jnp.float32
    ).astype(jnp.bfloat16)
    combine = jnp.where(dispatch, shares_here.T[:, None, :], 0.0)
    partial_rows = jnp.einsum(
        "esr,esd->rd", combine.astype(jnp.bfloat16), result, preferred_element_type=jnp.float32
    )
    moe_out = scatter_sum_ep(partial_rows.astype(jnp.bfloat16)).astype(jnp.bfloat16)
    return (attn_out, moe_out, new_cache)


def solution(mesh):
    in_specs = (
        P(("req", "ep"), None),
        P(("req", "ep")),
        P(("req", "ep"), None),
        P(("req", "ep"), None),
        P(),
        P(),
        P(None, "ep"),
        P(None, "ep"),
        P(None, "ep"),
        P("ep", None),
        P("ep", None, None),
        P("ep", None, None),
        P("req", "ep", None, None, None),
        P(),
    )
    out_specs = (P(("req", "ep"), None), P(("req", "ep"), None), P("req", "ep", None, None, None))
    return jax.shard_map(body, mesh=mesh, in_specs=in_specs, out_specs=out_specs, check_vma=False)
```

profile of v0, /device:TPU:24, one launch (start us, length us, event | category | flops | bytes accessed | tf_op | source)
XLA Modules:
  0.0 188.6 jit_solution(13958122429944967063)
XLA Ops:
  0.6 1.3 fusion.39
  1.9 1.2 fusion.41
  3.1 1.6 collective-permute-start
  4.6 1.3 broadcast_in_dim.43
  5.9 4.9 %all-to-all-start = ((s32[32,1,128]{2,1,0:T(1,128)}), s32[32,1,128]{2,1,0:T(1,128)S(1)}, u32[]{:S(2)}, u32[]{:S(2)}) async-start(s32[32,1,128]{2,1,0:T(1,128)} %broadcast_in_dim.43), calls=%async_computation | async-start | bytes 32768 | tf_op jit(solution)/shard_map/all_to_all | solution.py:55
  12.0 2.1 %collective-permute-done = bf16[128,1536]{1,0:T(8,128)(2,1)S(1)} collective-permute-done((bf16[128,1536]{1,0:T(8,128)(2,1)S(1)}, bf16[128,1536]{1,0:T(8,128)(2,1)S(1)}, u32[]{:S(2)}, u32[]{:S(2)}) %collective-permute-start) | collective-permute-done | bytes 393248 | tf_op jit(solution)/shard_map/ppermute | solution.py:84
  15.9 1.6 multiply_cosine_fusion
  17.5 1.6 maximum_select_fusion
  19.1 2.1 %gather_fusion = bf16[2,2,128,1536]{3,2,1,0:T(8,128)(2,1)} fusion(bf16[2,2,128,1536]{3,2,0,1:T(8,128)(2,1)S(1)} %maximum_select_fusion, s32[1024]{0:T(1024)} %pad_clamp_fusion), kind=kCustom, calls=%fused_computation | custom fusion | bytes 3145736 | tf_op jit(solution)/shard_map/jit(_take)/gather | solution.py:89
  21.2 3.1 %fusion.23 = f32[512,640]{1,0:T(8,128)S(1)} fusion(bf16[512,1536]{1,0:T(8,128)(2,1)} %bitcast.137, bf16[1536,128]{1,0:T(8,128)(2,1)S(1)} %copy-done.14, bf16[1536,128]{1,0:T(8,128)(2,1)S(1)} %copy-done.15, bf16[1536,384]{1,0:T(8,128)(2,1)} %param.20), kind=kOutput, calls=%fused_computation.18 | convolution fusion | flops 1012531200 | bytes 4849664 | tf_op jit(solution)/shard_map/dot_general | solution.py:221
  25.8 1.6 broadcast_in_dim.49
  27.4 6.6 %all-to-all-start.1 = ((bf16[8,4,512,64]{2,3,1,0:T(8,128)(2,1)}), bf16[8,4,512,64]{2,3,1,0:T(8,128)(2,1)S(1)}, u32[]{:S(2)}, u32[]{:S(2)}) async-start(bf16[8,4,512,64]{2,3,1,0:T(8,128)(2,1)} %broadcast_in_dim.49), calls=%async_computation.1 | async-start | bytes 4194304 | tf_op jit(solution)/shard_map/all_to_all | solution.py:250
  36.4 2.1 %slice.79 = f32[512,384]{1,0:T(8,128)} slice(f32[512,640]{1,0:T(8,128)} %copy-done.6), slice={[0:512], [0:384]} | slice | bytes 1572864 | tf_op jit(solution)/shard_map/slice | solution.py:230
  38.4 2.3 %copy.93 = f32[512,384]{0,1:T(8,128)} copy(f32[512,384]{1,0:T(8,128)} %slice.79) | data formatting | bytes 1572864 | tf_op jit(solution)/shard_map/slice | solution.py:230
  40.7 1.9 %subtract_convert_fusion = (bf16[512,6,32]{0,2,1:T(8,128)(2,1)}, bf16[512,6,32]{0,2,1:T(8,128)(2,1)S(1)}) fusion(f32[512,6,64]{0,2,1:T(8,128)} %bitcast.132, f32[512,32]{0,1:T(8,128)} %get-tuple-element.36, f32[512,32]{0,1:T(8,128)S(1)} %copy-done.8), kind=kLoop, calls=%fused_computation.61 | loop fusion | flops 786432 | bytes 1310720 | tf_op jit(solution)/shard_map/convert.8
  42.6 2.1 %copy.94 = bf16[512,6,32]{2,0,1:T(8,128)(2,1)} copy(bf16[512,6,32]{0,2,1:T(8,128)(2,1)} %get-tuple-element.25) | data formatting | bytes 393216 | tf_op jit(solution)/shard_map/convert.8
  45.9 2.7 %maximum_bitcast_fusion.q_ref = bf16[2,3,512,64]{3,2,1,0:T(8,128)(2,1)} fusion(bf16[512,2,3,32]{3,0,2,1:T(8,128)(2,1)} %bitcast.134, bf16[512,2,3,32]{3,0,2,1:T(8,128)(2,1)} %bitcast.133), kind=kLoop, calls=%fused_computation.46 | loop fusion | flops 786432 | bytes 786432 | tf_op jit(solution)/shard_map/transpose | solution.py:243
  48.6 32.3 %all-to-all-done.1 = bf16[8,4,512,64]{2,3,1,0:T(8,128)(2,1)S(1)} async-done(((bf16[8,4,512,64]{2,3,1,0:T(8,128)(2,1)}), bf16[8,4,512,64]{2,3,1,0:T(8,128)(2,1)S(1)}, u32[]{:S(2)}, u32[]{:S(2)}) %all-to-all-start.1) | async-done | bytes 2097184 | tf_op jit(solution)/shard_map/all_to_all | solution.py:250
  80.9 3.2 %copy.98.k_ref.v_ref = bf16[8,4,512,64]{3,2,1,0:T(8,128)(2,1)} copy(bf16[8,4,512,64]{2,3,1,0:T(8,128)(2,1)S(1)} %all-to-all-done.1) | data formatting | bytes 4194304 | tf_op jit(solution)/shard_map/all_to_all | solution.py:250
  84.1 21.2 %shard_map.157 = bf16[2,3,512,64]{3,2,1,0:T(8,128)(2,1)} custom-call(s32[2]{0:T(128)} %get-tuple-element.38.lo_ref, s32[2]{0:T(128)} %get-tuple-element.37.hi_ref, bf16[2,3,512,64]{3,2,1,0:T(8,128)(2,1)} %maximum_bitcast_fusion.q_ref, bf16[8,4,512,64]{3,2,1,0:T(8,128)(2,1)} %copy.98.k_ref.v_ref, bf16[8,4,512,64]{3,2,1,0:T(8,128)(2,1)} %copy.98.k_ref.v_ref, ...), custom_call_target="tpu_custom_call" | custom-call | tf_op jit(solution)/shard_map/pallas_call | solution.py:186
  105.3 2.2 %fusion.17 = bf16[512,1536]{1,0:T(8,128)(2,1)S(1)} fusion(bf16[2,3,512,64]{3,2,1,0:T(8,128)(2,1)} %shard_map.157, bf16[2,3,64,1536]{3,2,1,0:T(8,128)(2,1)S(1)} %bitcast.126), kind=kOutput, calls=%fused_computation.16 | convolution fusion | flops 604766208 | bytes 3145728 | tf_op jit(solution)/shard_map/grtd,grdo->to/dot_general | solution.py:270
  108.9 2.2 %collective-permute-done.2 = bf16[2,128,1536]{2,1,0:T(8,128)(2,1)S(1)} collective-permute-done((bf16[2,128,1536]{2,1,0:T(8,128)(2,1)S(1)}, bf16[2,128,1536]{2,1,0:T(8,128)(2,1)S(1)}, u32[]{:S(2)}, u32[]{:S(2)}) %collective-permute-start.2) | collective-permute-done | bytes 786464 | tf_op jit(solution)/shard_map/ppermute | solution.py:105
  111.1 1.7 convert_add_fusion.1
  113.5 10.6 %collective-permute-done.3 = bf16[128,1536]{1,0:T(8,128)(2,1)S(1)} collective-permute-done((bf16[128,1536]{1,0:T(8,128)(2,1)S(1)}, bf16[128,1536]{1,0:T(8,128)(2,1)S(1)}, u32[]{:S(2)}, u32[]{:S(2)}) %collective-permute-start.3) | collective-permute-done | bytes 393248 | tf_op jit(solution)/shard_map/ppermute | solution.py:110
  126.6 3.5 %all-to-all-start.2 = ((f32[4,128,40]{1,2,0:T(8,128)}), f32[4,128,40]{1,2,0:T(8,128)S(1)}, u32[]{:S(2)}, u32[]{:S(2)}) async-start(f32[4,128,40]{1,2,0:T(8,128)} %broadcast_in_dim.53), calls=%async_computation.2 | async-start | bytes 163840 | tf_op jit(solution)/shard_map/all_to_all | solution.py:55
  130.1 6.0 %collective-permute-done.4 = bf16[128,1536]{1,0:T(8,128)(2,1)S(1)} collective-permute-done((bf16[128,1536]{1,0:T(8,128)(2,1)S(1)}, bf16[128,1536]{1,0:T(8,128)(2,1)S(1)}, u32[]{:S(2)}, u32[]{:S(2)}) %collective-permute-start.4) | collective-permute-done | bytes 393248 | tf_op jit(solution)/shard_map/ppermute | solution.py:84
  137.3 1.3 collective-permute-done.5
  138.8 2.0 %gather_fusion.1 = bf16[2,2,128,1536]{3,2,1,0:T(8,128)(2,1)} fusion(bf16[2,2,128,1536]{3,2,0,1:T(8,128)(2,1)S(1)} %maximum_select_fusion.1, s32[1024]{0:T(1024)} %pad_clamp_fusion), kind=kCustom, calls=%fused_computation.1 | custom fusion | bytes 3145736 | tf_op jit(solution)/shard_map/jit(_take)/gather | solution.py:89
  140.8 17.3 %fusion.4 = f32[10,192,1024]{2,1,0:T(8,128)} fusion(bf16[10,1536,1024]{2,1,0:T(8,128)(2,1)} %param.24, bf16[512,1536,1]{1,0,2:T(8,128)(2,1)} %bitcast.136, s32[10,512]{1,0:T(8,128)S(1)} %copy.106, pred[10,512]{1,0:T(8,128)(4,1)S(1)} %get-tuple-element.21), kind=kOutput, calls=%fused_computation.6 | convolution fusion | flops 9064611840 | bytes 40920064 | tf_op jit(solution)/shard_map/esd,edf->esf/dot_general | solution.py:300
  158.1 14.5 %fusion.18 = bf16[512,1536]{1,0:T(8,128)(2,1)S(1)} fusion(bf16[10,512,1536]{2,1,0:T(8,128)(2,1)} %param.25, f32[10,192,1024]{2,1,0:T(8,128)} %fusion.4, bf16[10,512]{1,0:T(8,128)(2,1)S(1)} %dynamic-slice_bitcast_fusion, s32[10,512]{1,0:T(8,128)S(1)} %copy.106, pred[10,512]{1,0:T(8,128)(4,1)S(1)} %get-tuple-element.21), kind=kOutput, calls=%fused_computation.17 | convolution fusion | flops 6052380672 | bytes 25201664 | tf_op jit(solution)/shard_map/esr,esd->rd/dot_general | solution.py:308
  177.3 2.9 %gather_fusion.2 = bf16[12,2,2,64,64]{4,3,2,1,0:T(8,128)(2,1)S(1)} fusion(bf16[8,2,2,8,64,64]{5,4,3,2,1,0:T(8,128)(2,1)} %bitcast.127, s32[12]{0:T(128)S(1)} %fusion.52), kind=kCustom, calls=%fused_computation.2 | custom fusion | bytes 786528 | tf_op jit(solution)/shard_map/gather | solution.py:264
  181.4 6.4 %collective-permute-done.7 = bf16[128,1536]{1,0:T(8,128)(2,1)S(1)} collective-permute-done((bf16[128,1536]{1,0:T(8,128)(2,1)S(1)}, bf16[128,1536]{1,0:T(8,128)(2,1)S(1)}, u32[]{:S(2)}, u32[]{:S(2)}) %collective-permute-start.7) | collective-permute-done | bytes 393248 | tf_op jit(solution)/shard_map/ppermute | solution.py:110
  (98 shorter events, 20.4 us)
Async XLA Ops:
  0.6 104.7 %copy-start = (bf16[384,1536]{1,0:T(8,128)(2,1)S(1)}, bf16[384,1536]{1,0:T(8,128)(2,1)}, u32[]{:S(2)}) copy-start(bf16[384,1536]{1,0:T(8,128)(2,1)} %param.23) | copy-start | bytes 3538948
  3.1 11.1 %collective-permute-start = (bf16[128,1536]{1,0:T(8,128)(2,1)S(1)}, bf16[128,1536]{1,0:T(8,128)(2,1)S(1)}, u32[]{:S(2)}, u32[]{:S(2)}) collective-permute-start(bf16[128,1536]{1,0:T(8,128)(2,1)S(1)} %fusion.41), channel_id=1, source_target_pairs={{0,2},{1,3},{2,0},{3,1},{4,6},{5,7},{6,4},{7,5},{8,10},{9,11},{10,... | collective-permute-start | bytes 1179656 | tf_op jit(solution)/shard_map/ppermute | solution.py:84
  5.9 9.2 %all-to-all-start = ((s32[32,1,128]{2,1,0:T(1,128)}), s32[32,1,128]{2,1,0:T(1,128)S(1)}, u32[]{:S(2)}, u32[]{:S(2)}) async-start(s32[32,1,128]{2,1,0:T(1,128)} %broadcast_in_dim.43), calls=%async_computation | async-start | bytes 32768 | tf_op jit(solution)/shard_map/all_to_all | solution.py:55
  14.3 3.2 %collective-permute-start.1 = (bf16[2,128,1536]{2,1,0:T(8,128)(2,1)S(1)}, bf16[2,128,1536]{2,1,0:T(8,128)(2,1)}, u32[]{:S(2)}, u32[]{:S(2)}) collective-permute-start(bf16[2,128,1536]{2,1,0:T(8,128)(2,1)S(1)} %get-tuple-element.30), channel_id=1, source_target_pairs={{0,1},{1,0},{2,3},{3,2},{4,5},{5,4},{6,7},{7,6},{8,9},{9,8},{10,11... | collective-permute-start | bytes 2359304 | tf_op jit(solution)/shard_map/ppermute | solution.py:86
  19.1 2.1 %copy-start.14 = (bf16[1536,128]{1,0:T(8,128)(2,1)S(1)}, bf16[1536,128]{1,0:T(8,128)(2,1)}, u32[]{:S(2)}) copy-start(bf16[1536,128]{1,0:T(8,128)(2,1)} %param.22) | copy-start | bytes 1179652
  19.1 2.1 %copy-start.15 = (bf16[1536,128]{1,0:T(8,128)(2,1)S(1)}, bf16[1536,128]{1,0:T(8,128)(2,1)}, u32[]{:S(2)}) copy-start(bf16[1536,128]{1,0:T(8,128)(2,1)} %param.21) | copy-start | bytes 1179652
  24.3 1.1 copy-start.6
  24.3 1.3 copy-start.8
  24.3 1.3 copy-start.9
  27.4 53.6 %all-to-all-start.1 = ((bf16[8,4,512,64]{2,3,1,0:T(8,128)(2,1)}), bf16[8,4,512,64]{2,3,1,0:T(8,128)(2,1)S(1)}, u32[]{:S(2)}, u32[]{:S(2)}) async-start(bf16[8,4,512,64]{2,3,1,0:T(8,128)(2,1)} %broadcast_in_dim.49), calls=%async_computation.1 | async-start | bytes 4194304 | tf_op jit(solution)/shard_map/all_to_all | solution.py:250
  107.5 1.2 copy-start.2
  108.7 2.4 %collective-permute-start.2 = (bf16[2,128,1536]{2,1,0:T(8,128)(2,1)S(1)}, bf16[2,128,1536]{2,1,0:T(8,128)(2,1)S(1)}, u32[]{:S(2)}, u32[]{:S(2)}) collective-permute-start(bf16[2,128,1536]{2,1,0:T(8,128)(2,1)S(1)} %select_bitcast_fusion.1), channel_id=1, source_target_pairs={{0,1},{1,0},{2,3},{3,2},{4,5},{5,4},{6,7},{7,6},{8,9},{9,8},{10,11... | collective-permute-start | bytes 2359304 | tf_op jit(solution)/shard_map/ppermute | solution.py:105
  108.8 15.2 %copy-start.3 = (bf16[128,1536]{1,0:T(8,128)(2,1)S(1)}, bf16[128,1536]{1,0:T(8,128)(2,1)}, u32[]{:S(2)}) copy-start(bf16[128,1536]{1,0:T(8,128)(2,1)} %param.14) | copy-start | bytes 1179652
  112.8 11.6 %copy-start.10 = (f32[1536]{0:T(1024)S(1)}, f32[1536]{0:T(1024)}, u32[]{:S(2)}) copy-start(f32[1536]{0:T(1024)} %param.19) | copy-start | bytes 18436
  112.8 11.2 %collective-permute-start.3 = (bf16[128,1536]{1,0:T(8,128)(2,1)S(1)}, bf16[128,1536]{1,0:T(8,128)(2,1)S(1)}, u32[]{:S(2)}, u32[]{:S(2)}) collective-permute-start(bf16[128,1536]{1,0:T(8,128)(2,1)S(1)} %fusion.43), channel_id=1, source_target_pairs={{0,2},{1,3},{2,0},{3,1},{4,6},{5,7},{6,4},{7,5},{8,10},{9,11},{10,... | collective-permute-start | bytes 1179656 | tf_op jit(solution)/shard_map/ppermute | solution.py:110
  124.3 1.6 copy-start.11
  124.3 1.6 copy-start.12
  125.3 10.8 %collective-permute-start.4 = (bf16[128,1536]{1,0:T(8,128)(2,1)S(1)}, bf16[128,1536]{1,0:T(8,128)(2,1)S(1)}, u32[]{:S(2)}, u32[]{:S(2)}) collective-permute-start(bf16[128,1536]{1,0:T(8,128)(2,1)S(1)} %get-tuple-element.23), channel_id=1, source_target_pairs={{0,2},{1,3},{2,0},{3,1},{4,6},{5,7},{6,4},{7,5},{8,10},{9,11},{10,... | collective-permute-start | bytes 1179656 | tf_op jit(solution)/shard_map/ppermute | solution.py:84
  126.6 10.0 %all-to-all-start.2 = ((f32[4,128,40]{1,2,0:T(8,128)}), f32[4,128,40]{1,2,0:T(8,128)S(1)}, u32[]{:S(2)}, u32[]{:S(2)}) async-start(f32[4,128,40]{1,2,0:T(8,128)} %broadcast_in_dim.53), calls=%async_computation.2 | async-start | bytes 163840 | tf_op jit(solution)/shard_map/all_to_all | solution.py:55
  136.2 2.4 %collective-permute-start.5 = (bf16[2,128,1536]{2,1,0:T(8,128)(2,1)S(1)}, bf16[2,128,1536]{2,1,0:T(8,128)(2,1)S(1)}, u32[]{:S(2)}, u32[]{:S(2)}) collective-permute-start(bf16[2,128,1536]{2,1,0:T(8,128)(2,1)S(1)} %get-tuple-element.28), channel_id=1, source_target_pairs={{0,1},{1,0},{2,3},{3,2},{4,5},{5,4},{6,7},{7,6},{8,9},{9,8},{10,11... | collective-permute-start | bytes 2359304 | tf_op jit(solution)/shard_map/ppermute | solution.py:86
  172.6 0.7 copy-start.13
  172.7 2.4 %collective-permute-start.6 = (bf16[2,128,1536]{2,1,0:T(8,128)(2,1)S(1)}, bf16[2,128,1536]{2,1,0:T(8,128)(2,1)S(1)}, u32[]{:S(2)}, u32[]{:S(2)}) collective-permute-start(bf16[2,128,1536]{2,1,0:T(8,128)(2,1)S(1)} %select_bitcast_fusion), channel_id=1, source_target_pairs={{0,1},{1,0},{2,3},{3,2},{4,5},{5,4},{6,7},{7,6},{8,9},{9,8},{10,11... | collective-permute-start | bytes 2359304 | tf_op jit(solution)/shard_map/ppermute | solution.py:105
  175.3 1.2 copy-start.4
  176.5 3.8 %copy-start.7 = (bf16[12,2,2,64,64]{4,3,2,1,0:T(8,128)(2,1)S(1)}, bf16[12,2,2,64,64]{4,3,2,1,0:T(8,128)(2,1)}, u32[]{:S(2)}) copy-start(bf16[12,2,2,64,64]{4,3,2,1,0:T(8,128)(2,1)} %param.26) | copy-start | bytes 1179652
  176.5 11.2 %collective-permute-start.7 = (bf16[128,1536]{1,0:T(8,128)(2,1)S(1)}, bf16[128,1536]{1,0:T(8,128)(2,1)S(1)}, u32[]{:S(2)}, u32[]{:S(2)}) collective-permute-start(bf16[128,1536]{1,0:T(8,128)(2,1)S(1)} %fusion.44), channel_id=1, source_target_pairs={{0,2},{1,3},{2,0},{3,1},{4,6},{5,7},{6,4},{7,5},{8,10},{9,11},{10,... | collective-permute-start | bytes 1179656 | tf_op jit(solution)/shard_map/ppermute | solution.py:110
  180.3 7.5 %copy-start.5 = (f32[2,128,1536]{2,1,0:T(8,128)S(1)}, f32[2,128,1536]{2,1,0:T(8,128)}, u32[]{:S(2)}) copy-start(f32[2,128,1536]{2,1,0:T(8,128)} %copy-done.4) | copy-start | bytes 4718596
  180.3 8.3 %copy-start.1 = (bf16[384,1536]{1,0:T(8,128)(2,1)S(1)}, bf16[384,1536]{1,0:T(8,128)(2,1)}, u32[]{:S(2)}) copy-start(bf16[384,1536]{1,0:T(8,128)(2,1)} %param.23) | copy-start | bytes 3538948
where the time goes:
time: 191 us; the launch traced here: 189 us
  waiting for transfers between devices  63 us (33%)
  matrix products  37 us (19%)
  local copies, waits for them, and re-layouts  27.7 us (15%)
  Pallas kernels  21.2 us (11%)
  other arithmetic  19.7 us (10%)
  starting transfers between devices  18.8 us (10%)
    all_to_all x1, waiting for transfers between devices, body(): lax.all_to_all(jnp.broadcast_to(kv_local[None], (req_count,) + kv_local.s...  32.3 us
    pallas_call x1, Pallas kernels, flash_attention(): pl.pallas_call(flash_body, grid_spec=grid_spec, out_shape=jax.ShapeDtypeS...  21.2 us
    dot_general x1, matrix products, body(): jnp.einsum('esd,edf->esf', arrived, w_in, preferred_element_type=jnp.floa...  17.3 us
    ppermute x2, waiting for transfers between devices, scatter_sum_ep(): lax.ppermute(piece.astype(jnp.bfloat16), 'ep', chip_pairs(count, shift))  16.9 us
    dot_general x1, matrix products, body(): jnp.einsum('esr,esd->rd', combine.astype(jnp.bfloat16), result, preferred...  14.5 us
    all_to_all x2, starting transfers between devices, gather_rows(): got = lax.all_to_all(spread, axis_name, 0, 0, tiled=True)  8.42 us
    ppermute x2, waiting for transfers between devices, gather_ep(): side.append(lax.ppermute(x, 'ep', chip_pairs(count, shift)))  8.1 us
    all_to_all x1, starting transfers between devices, body(): lax.all_to_all(jnp.broadcast_to(kv_local[None], (req_count,) + kv_local.s...  6.57 us
  transfers between devices with their start and end apart: 11, of which 10 were waited for; matrix products, arithmetic and copies ran while one was open for 14% of the time, Pallas kernels for 0%

commit v1 on v0

--- a/solution.py
+++ b/solution.py
@@ -113,7 +113,7 @@
     return total
 
 
-Q_TILE = 256
+Q_TILE = 512
 K_TILE = 512
 
 

time: 191 us -> 189 us (0.990)
  the two profiles are of different devices: /device:TPU:24 before, /device:TPU:12 now
where the time goes in v1:
time: 189 us; the launch traced here: 186 us
  waiting for transfers between devices  57.5 us (30%)
  matrix products  37 us (20%)
  local copies, waits for them, and re-layouts  27.7 us (15%)
  Pallas kernels  20 us (11%)
  other arithmetic  19.5 us (10%)
  starting transfers between devices  18.3 us (10%)
  between operations  6.28 us (3%)
    all_to_all x1, waiting for transfers between devices, body(): lax.all_to_all(jnp.broadcast_to(kv_local[None], (req_count,) + kv_local.s...  26.2 us
    pallas_call x1, Pallas kernels, flash_attention(): pl.pallas_call(flash_body, grid_spec=grid_spec, out_shape=jax.ShapeDtypeS...  20 us
    dot_general x1, matrix products, body(): jnp.einsum('esd,edf->esf', arrived, w_in, preferred_element_type=jnp.floa...  17.3 us
    ppermute x2, waiting for transfers between devices, scatter_sum_ep(): lax.ppermute(piece.astype(jnp.bfloat16), 'ep', chip_pairs(count, shift))  16.9 us
    dot_general x1, matrix products, body(): jnp.einsum('esr,esd->rd', combine.astype(jnp.bfloat16), result, preferred...  14.5 us
    all_to_all x2, starting transfers between devices, gather_rows(): got = lax.all_to_all(spread, axis_name, 0, 0, tiled=True)  8.54 us
    ppermute x2, waiting for transfers between devices, gather_ep(): side.append(lax.ppermute(x, 'ep', chip_pairs(count, shift)))  7.85 us
    all_to_all x1, starting transfers between devices, body(): lax.all_to_all(jnp.broadcast_to(kv_local[None], (req_count,) + kv_local.s...  5.89 us
  transfers between devices with their start and end apart: 11, of which 10 were waited for; matrix products, arithmetic and copies ran while one was open for 14% of the time, Pallas kernels for 0%

profile of v1, /device:TPU:12, one launch (start us, length us, event | category | flops | bytes accessed | tf_op | source)
XLA Modules:
  0.0 186.3 jit_solution(14023877442104827044)
XLA Ops:
  0.6 1.3 fusion.39
  3.1 1.6 collective-permute-start
  4.6 1.3 broadcast_in_dim.43
  5.9 5.1 %all-to-all-start = ((s32[32,1,128]{2,1,0:T(1,128)}), s32[32,1,128]{2,1,0:T(1,128)S(1)}, u32[]{:S(2)}, u32[]{:S(2)}) async-start(s32[32,1,128]{2,1,0:T(1,128)} %broadcast_in_dim.43), calls=%async_computation | async-start | bytes 32768 | tf_op jit(solution)/shard_map/all_to_all | solution.py:55
  12.1 1.9 %collective-permute-done = bf16[128,1536]{1,0:T(8,128)(2,1)S(1)} collective-permute-done((bf16[128,1536]{1,0:T(8,128)(2,1)S(1)}, bf16[128,1536]{1,0:T(8,128)(2,1)S(1)}, u32[]{:S(2)}, u32[]{:S(2)}) %collective-permute-start) | collective-permute-done | bytes 393248 | tf_op jit(solution)/shard_map/ppermute | solution.py:84
  14.2 1.7 all-to-all-done
  17.3 1.6 multiply_cosine_fusion
  18.9 1.6 maximum_select_fusion
  20.5 2.1 %gather_fusion = bf16[2,2,128,1536]{3,2,1,0:T(8,128)(2,1)} fusion(bf16[2,2,128,1536]{3,2,0,1:T(8,128)(2,1)S(1)} %maximum_select_fusion, s32[1024]{0:T(1024)} %pad_clamp_fusion), kind=kCustom, calls=%fused_computation | custom fusion | bytes 3145736 | tf_op jit(solution)/shard_map/jit(_take)/gather | solution.py:89
  22.6 3.1 %fusion.23 = f32[512,640]{1,0:T(8,128)S(1)} fusion(bf16[512,1536]{1,0:T(8,128)(2,1)} %bitcast.139, bf16[1536,128]{1,0:T(8,128)(2,1)S(1)} %copy-done.14, bf16[1536,128]{1,0:T(8,128)(2,1)S(1)} %copy-done.15, bf16[1536,384]{1,0:T(8,128)(2,1)} %param.20), kind=kOutput, calls=%fused_computation.18 | convolution fusion | flops 1012531200 | bytes 4849664 | tf_op jit(solution)/shard_map/dot_general | solution.py:221
  27.2 1.6 broadcast_in_dim.49
  28.8 5.9 %all-to-all-start.1 = ((bf16[8,4,512,64]{2,3,1,0:T(8,128)(2,1)}), bf16[8,4,512,64]{2,3,1,0:T(8,128)(2,1)S(1)}, u32[]{:S(2)}, u32[]{:S(2)}) async-start(bf16[8,4,512,64]{2,3,1,0:T(8,128)(2,1)} %broadcast_in_dim.49), calls=%async_computation.1 | async-start | bytes 4194304 | tf_op jit(solution)/shard_map/all_to_all | solution.py:250
  41.4 2.1 %slice.79 = f32[512,384]{1,0:T(8,128)} slice(f32[512,640]{1,0:T(8,128)} %copy-done.6), slice={[0:512], [0:384]} | slice | bytes 1572864 | tf_op jit(solution)/shard_map/slice | solution.py:230
  43.5 2.3 %copy.93 = f32[512,384]{0,1:T(8,128)} copy(f32[512,384]{1,0:T(8,128)} %slice.79) | data formatting | bytes 1572864 | tf_op jit(solution)/shard_map/slice | solution.py:230
  45.8 1.9 %subtract_convert_fusion = (bf16[512,6,32]{0,2,1:T(8,128)(2,1)}, bf16[512,6,32]{0,2,1:T(8,128)(2,1)S(1)}) fusion(f32[512,6,64]{0,2,1:T(8,128)} %bitcast.134, f32[512,32]{0,1:T(8,128)} %get-tuple-element.37, f32[512,32]{0,1:T(8,128)S(1)} %copy-done.8), kind=kLoop, calls=%fused_computation.61 | loop fusion | flops 786432 | bytes 1310720 | tf_op jit(solution)/shard_map/convert.8
  47.7 2.1 %copy.94 = bf16[512,6,32]{2,0,1:T(8,128)(2,1)} copy(bf16[512,6,32]{0,2,1:T(8,128)(2,1)} %get-tuple-element.27) | data formatting | bytes 393216 | tf_op jit(solution)/shard_map/convert.8
  51.0 2.7 %maximum_bitcast_fusion.q_ref = bf16[2,3,512,64]{3,2,1,0:T(8,128)(2,1)} fusion(bf16[512,2,3,32]{3,0,2,1:T(8,128)(2,1)} %bitcast.136, bf16[512,2,3,32]{3,0,2,1:T(8,128)(2,1)} %bitcast.135), kind=kLoop, calls=%fused_computation.46 | loop fusion | flops 786432 | bytes 786432 | tf_op jit(solution)/shard_map/transpose | solution.py:243
  53.7 26.2 %all-to-all-done.1 = bf16[8,4,512,64]{2,3,1,0:T(8,128)(2,1)S(1)} async-done(((bf16[8,4,512,64]{2,3,1,0:T(8,128)(2,1)}), bf16[8,4,512,64]{2,3,1,0:T(8,128)(2,1)S(1)}, u32[]{:S(2)}, u32[]{:S(2)}) %all-to-all-start.1) | async-done | bytes 2097184 | tf_op jit(solution)/shard_map/all_to_all | solution.py:250
  79.9 3.2 %copy.98.k_ref.v_ref = bf16[8,4,512,64]{3,2,1,0:T(8,128)(2,1)} copy(bf16[8,4,512,64]{2,3,1,0:T(8,128)(2,1)S(1)} %all-to-all-done.1) | data formatting | bytes 4194304 | tf_op jit(solution)/shard_map/all_to_all | solution.py:250
  83.1 20.0 %shard_map.157 = bf16[2,3,512,64]{3,2,1,0:T(8,128)(2,1)} custom-call(s32[1]{0:T(128)S(6)} %select_n.146.lo_ref, s32[1]{0:T(128)S(6)} %select_n.147.hi_ref, bf16[2,3,512,64]{3,2,1,0:T(8,128)(2,1)} %maximum_bitcast_fusion.q_ref, bf16[8,4,512,64]{3,2,1,0:T(8,128)(2,1)} %copy.98.k_ref.v_ref, bf16[8,4,512,64]{3,2,1,0:T(8,128)(2,1)} %copy.98.k_ref.v_ref, ...), custom_call_target="tpu_custom_call" | custom-call | tf_op jit(solution)/shard_map/pallas_call | solution.py:186
  103.1 2.2 %fusion.17 = bf16[512,1536]{1,0:T(8,128)(2,1)S(1)} fusion(bf16[2,3,512,64]{3,2,1,0:T(8,128)(2,1)} %shard_map.157, bf16[2,3,64,1536]{3,2,1,0:T(8,128)(2,1)S(1)} %bitcast.128), kind=kOutput, calls=%fused_computation.16 | convolution fusion | flops 604766208 | bytes 3145728 | tf_op jit(solution)/shard_map/grtd,grdo->to/dot_general | solution.py:270
  106.6 2.2 %collective-permute-done.2 = bf16[2,128,1536]{2,1,0:T(8,128)(2,1)S(1)} collective-permute-done((bf16[2,128,1536]{2,1,0:T(8,128)(2,1)S(1)}, bf16[2,128,1536]{2,1,0:T(8,128)(2,1)S(1)}, u32[]{:S(2)}, u32[]{:S(2)}) %collective-permute-start.2) | collective-permute-done | bytes 786464 | tf_op jit(solution)/shard_map/ppermute | solution.py:105
  108.9 1.7 convert_add_fusion.1
  111.3 10.6 %collective-permute-done.3 = bf16[128,1536]{1,0:T(8,128)(2,1)S(1)} collective-permute-done((bf16[128,1536]{1,0:T(8,128)(2,1)S(1)}, bf16[128,1536]{1,0:T(8,128)(2,1)S(1)}, u32[]{:S(2)}, u32[]{:S(2)}) %collective-permute-start.3) | collective-permute-done | bytes 393248 | tf_op jit(solution)/shard_map/ppermute | solution.py:110
  124.4 3.5 %all-to-all-start.2 = ((f32[4,128,40]{1,2,0:T(8,128)}), f32[4,128,40]{1,2,0:T(8,128)S(1)}, u32[]{:S(2)}, u32[]{:S(2)}) async-start(f32[4,128,40]{1,2,0:T(8,128)} %broadcast_in_dim.53), calls=%async_computation.2 | async-start | bytes 163840 | tf_op jit(solution)/shard_map/all_to_all | solution.py:55
  127.9 5.9 %collective-permute-done.4 = bf16[128,1536]{1,0:T(8,128)(2,1)S(1)} collective-permute-done((bf16[128,1536]{1,0:T(8,128)(2,1)S(1)}, bf16[128,1536]{1,0:T(8,128)(2,1)S(1)}, u32[]{:S(2)}, u32[]{:S(2)}) %collective-permute-start.4) | collective-permute-done | bytes 393248 | tf_op jit(solution)/shard_map/ppermute | solution.py:84
  135.0 1.3 collective-permute-done.5
  136.6 2.0 %gather_fusion.1 = bf16[2,2,128,1536]{3,2,1,0:T(8,128)(2,1)} fusion(bf16[2,2,128,1536]{3,2,0,1:T(8,128)(2,1)S(1)} %maximum_select_fusion.1, s32[1024]{0:T(1024)} %pad_clamp_fusion), kind=kCustom, calls=%fused_computation.1 | custom fusion | bytes 3145736 | tf_op jit(solution)/shard_map/jit(_take)/gather | solution.py:89
  138.6 17.3 %fusion.4 = f32[10,192,1024]{2,1,0:T(8,128)} fusion(bf16[10,1536,1024]{2,1,0:T(8,128)(2,1)} %param.24, bf16[512,1536,1]{1,0,2:T(8,128)(2,1)} %bitcast.138, s32[10,512]{1,0:T(8,128)S(1)} %copy.106, pred[10,512]{1,0:T(8,128)(4,1)S(1)} %get-tuple-element.21), kind=kOutput, calls=%fused_computation.6 | convolution fusion | flops 9064611840 | bytes 40920064 | tf_op jit(solution)/shard_map/esd,edf->esf/dot_general | solution.py:300
  155.9 14.5 %fusion.18 = bf16[512,1536]{1,0:T(8,128)(2,1)S(1)} fusion(bf16[10,512,1536]{2,1,0:T(8,128)(2,1)} %param.25, f32[10,192,1024]{2,1,0:T(8,128)} %fusion.4, bf16[10,512]{1,0:T(8,128)(2,1)S(1)} %dynamic-slice_bitcast_fusion, s32[10,512]{1,0:T(8,128)S(1)} %copy.106, pred[10,512]{1,0:T(8,128)(4,1)S(1)} %get-tuple-element.21), kind=kOutput, calls=%fused_computation.17 | convolution fusion | flops 6052380672 | bytes 25201664 | tf_op jit(solution)/shard_map/esr,esd->rd/dot_general | solution.py:308
  175.2 2.9 %gather_fusion.2 = bf16[12,2,2,64,64]{4,3,2,1,0:T(8,128)(2,1)S(1)} fusion(bf16[8,2,2,8,64,64]{5,4,3,2,1,0:T(8,128)(2,1)} %bitcast.129, s32[12]{0:T(128)S(1)} %fusion.54), kind=kCustom, calls=%fused_computation.2 | custom fusion | bytes 786528 | tf_op jit(solution)/shard_map/gather | solution.py:264
  179.2 6.3 %collective-permute-done.7 = bf16[128,1536]{1,0:T(8,128)(2,1)S(1)} collective-permute-done((bf16[128,1536]{1,0:T(8,128)(2,1)S(1)}, bf16[128,1536]{1,0:T(8,128)(2,1)S(1)}, u32[]{:S(2)}, u32[]{:S(2)}) %collective-permute-start.7) | collective-permute-done | bytes 393248 | tf_op jit(solution)/shard_map/ppermute | solution.py:110
  (94 shorter events, 20.7 us)
Async XLA Ops:
  0.6 102.5 %copy-start = (bf16[384,1536]{1,0:T(8,128)(2,1)S(1)}, bf16[384,1536]{1,0:T(8,128)(2,1)}, u32[]{:S(2)}) copy-start(bf16[384,1536]{1,0:T(8,128)(2,1)} %param.23) | copy-start | bytes 3538948
  3.1 11.0 %collective-permute-start = (bf16[128,1536]{1,0:T(8,128)(2,1)S(1)}, bf16[128,1536]{1,0:T(8,128)(2,1)S(1)}, u32[]{:S(2)}, u32[]{:S(2)}) collective-permute-start(bf16[128,1536]{1,0:T(8,128)(2,1)S(1)} %fusion.41), channel_id=1, source_target_pairs={{0,2},{1,3},{2,0},{3,1},{4,6},{5,7},{6,4},{7,5},{8,10},{9,11},{10,... | collective-permute-start | bytes 1179656 | tf_op jit(solution)/shard_map/ppermute | solution.py:84
  5.9 10.0 %all-to-all-start = ((s32[32,1,128]{2,1,0:T(1,128)}), s32[32,1,128]{2,1,0:T(1,128)S(1)}, u32[]{:S(2)}, u32[]{:S(2)}) async-start(s32[32,1,128]{2,1,0:T(1,128)} %broadcast_in_dim.43), calls=%async_computation | async-start | bytes 32768 | tf_op jit(solution)/shard_map/all_to_all | solution.py:55
  14.2 4.7 %collective-permute-start.1 = (bf16[2,128,1536]{2,1,0:T(8,128)(2,1)S(1)}, bf16[2,128,1536]{2,1,0:T(8,128)(2,1)}, u32[]{:S(2)}, u32[]{:S(2)}) collective-permute-start(bf16[2,128,1536]{2,1,0:T(8,128)(2,1)S(1)} %get-tuple-element.32), channel_id=1, source_target_pairs={{0,1},{1,0},{2,3},{3,2},{4,5},{5,4},{6,7},{7,6},{8,9},{9,8},{10,11... | collective-permute-start | bytes 2359304 | tf_op jit(solution)/shard_map/ppermute | solution.py:86
  20.5 2.1 %copy-start.14 = (bf16[1536,128]{1,0:T(8,128)(2,1)S(1)}, bf16[1536,128]{1,0:T(8,128)(2,1)}, u32[]{:S(2)}) copy-start(bf16[1536,128]{1,0:T(8,128)(2,1)} %param.22) | copy-start | bytes 1179652
  20.5 2.1 %copy-start.15 = (bf16[1536,128]{1,0:T(8,128)(2,1)S(1)}, bf16[1536,128]{1,0:T(8,128)(2,1)}, u32[]{:S(2)}) copy-start(bf16[1536,128]{1,0:T(8,128)(2,1)} %param.21) | copy-start | bytes 1179652
  25.7 1.1 copy-start.6
  25.7 1.3 copy-start.8
  25.7 1.3 copy-start.9
  28.8 51.2 %all-to-all-start.1 = ((bf16[8,4,512,64]{2,3,1,0:T(8,128)(2,1)}), bf16[8,4,512,64]{2,3,1,0:T(8,128)(2,1)S(1)}, u32[]{:S(2)}, u32[]{:S(2)}) async-start(bf16[8,4,512,64]{2,3,1,0:T(8,128)(2,1)} %broadcast_in_dim.49), calls=%async_computation.1 | async-start | bytes 4194304 | tf_op jit(solution)/shard_map/all_to_all | solution.py:250
  105.3 1.2 copy-start.2
  106.5 2.4 %collective-permute-start.2 = (bf16[2,128,1536]{2,1,0:T(8,128)(2,1)S(1)}, bf16[2,128,1536]{2,1,0:T(8,128)(2,1)S(1)}, u32[]{:S(2)}, u32[]{:S(2)}) collective-permute-start(bf16[2,128,1536]{2,1,0:T(8,128)(2,1)S(1)} %select_bitcast_fusion.1), channel_id=1, source_target_pairs={{0,1},{1,0},{2,3},{3,2},{4,5},{5,4},{6,7},{7,6},{8,9},{9,8},{10,11... | collective-permute-start | bytes 2359304 | tf_op jit(solution)/shard_map/ppermute | solution.py:105
  106.6 15.2 %copy-start.3 = (bf16[128,1536]{1,0:T(8,128)(2,1)S(1)}, bf16[128,1536]{1,0:T(8,128)(2,1)}, u32[]{:S(2)}) copy-start(bf16[128,1536]{1,0:T(8,128)(2,1)} %param.14) | copy-start | bytes 1179652
  110.5 11.6 %copy-start.10 = (f32[1536]{0:T(1024)S(1)}, f32[1536]{0:T(1024)}, u32[]{:S(2)}) copy-start(f32[1536]{0:T(1024)} %param.19) | copy-start | bytes 18436
  110.6 11.2 %collective-permute-start.3 = (bf16[128,1536]{1,0:T(8,128)(2,1)S(1)}, bf16[128,1536]{1,0:T(8,128)(2,1)S(1)}, u32[]{:S(2)}, u32[]{:S(2)}) collective-permute-start(bf16[128,1536]{1,0:T(8,128)(2,1)S(1)} %fusion.43), channel_id=1, source_target_pairs={{0,2},{1,3},{2,0},{3,1},{4,6},{5,7},{6,4},{7,5},{8,10},{9,11},{10,... | collective-permute-start | bytes 1179656 | tf_op jit(solution)/shard_map/ppermute | solution.py:110
  122.1 1.6 copy-start.11
  122.1 1.6 copy-start.12
  123.1 10.8 %collective-permute-start.4 = (bf16[128,1536]{1,0:T(8,128)(2,1)S(1)}, bf16[128,1536]{1,0:T(8,128)(2,1)S(1)}, u32[]{:S(2)}, u32[]{:S(2)}) collective-permute-start(bf16[128,1536]{1,0:T(8,128)(2,1)S(1)} %get-tuple-element.25), channel_id=1, source_target_pairs={{0,2},{1,3},{2,0},{3,1},{4,6},{5,7},{6,4},{7,5},{8,10},{9,11},{10,... | collective-permute-start | bytes 1179656 | tf_op jit(solution)/shard_map/ppermute | solution.py:84
  124.4 9.9 %all-to-all-start.2 = ((f32[4,128,40]{1,2,0:T(8,128)}), f32[4,128,40]{1,2,0:T(8,128)S(1)}, u32[]{:S(2)}, u32[]{:S(2)}) async-start(f32[4,128,40]{1,2,0:T(8,128)} %broadcast_in_dim.53), calls=%async_computation.2 | async-start | bytes 163840 | tf_op jit(solution)/shard_map/all_to_all | solution.py:55
  134.0 2.4 %collective-permute-start.5 = (bf16[2,128,1536]{2,1,0:T(8,128)(2,1)S(1)}, bf16[2,128,1536]{2,1,0:T(8,128)(2,1)S(1)}, u32[]{:S(2)}, u32[]{:S(2)}) collective-permute-start(bf16[2,128,1536]{2,1,0:T(8,128)(2,1)S(1)} %get-tuple-element.30), channel_id=1, source_target_pairs={{0,1},{1,0},{2,3},{3,2},{4,5},{5,4},{6,7},{7,6},{8,9},{9,8},{10,11... | collective-permute-start | bytes 2359304 | tf_op jit(solution)/shard_map/ppermute | solution.py:86
  170.4 0.7 copy-start.13
  170.5 2.4 %collective-permute-start.6 = (bf16[2,128,1536]{2,1,0:T(8,128)(2,1)S(1)}, bf16[2,128,1536]{2,1,0:T(8,128)(2,1)S(1)}, u32[]{:S(2)}, u32[]{:S(2)}) collective-permute-start(bf16[2,128,1536]{2,1,0:T(8,128)(2,1)S(1)} %select_bitcast_fusion), channel_id=1, source_target_pairs={{0,1},{1,0},{2,3},{3,2},{4,5},{5,4},{6,7},{7,6},{8,9},{9,8},{10,11... | collective-permute-start | bytes 2359304 | tf_op jit(solution)/shard_map/ppermute | solution.py:105
  173.1 1.2 copy-start.4
  174.3 3.8 %copy-start.7 = (bf16[12,2,2,64,64]{4,3,2,1,0:T(8,128)(2,1)S(1)}, bf16[12,2,2,64,64]{4,3,2,1,0:T(8,128)(2,1)}, u32[]{:S(2)}) copy-start(bf16[12,2,2,64,64]{4,3,2,1,0:T(8,128)(2,1)} %param.26) | copy-start | bytes 1179652
  174.3 11.2 %collective-permute-start.7 = (bf16[128,1536]{1,0:T(8,128)(2,1)S(1)}, bf16[128,1536]{1,0:T(8,128)(2,1)S(1)}, u32[]{:S(2)}, u32[]{:S(2)}) collective-permute-start(bf16[128,1536]{1,0:T(8,128)(2,1)S(1)} %fusion.44), channel_id=1, source_target_pairs={{0,2},{1,3},{2,0},{3,1},{4,6},{5,7},{6,4},{7,5},{8,10},{9,11},{10,... | collective-permute-start | bytes 1179656 | tf_op jit(solution)/shard_map/ppermute | solution.py:110
  178.1 7.5 %copy-start.5 = (f32[2,128,1536]{2,1,0:T(8,128)S(1)}, f32[2,128,1536]{2,1,0:T(8,128)}, u32[]{:S(2)}) copy-start(f32[2,128,1536]{2,1,0:T(8,128)} %copy-done.4) | copy-start | bytes 4718596
  178.1 8.3 %copy-start.1 = (bf16[384,1536]{1,0:T(8,128)(2,1)S(1)}, bf16[384,1536]{1,0:T(8,128)(2,1)}, u32[]{:S(2)}) copy-start(bf16[384,1536]{1,0:T(8,128)(2,1)} %param.23) | copy-start | bytes 3538948

commit v2 on v0

--- a/solution.py
+++ b/solution.py
@@ -117,7 +117,7 @@
 K_TILE = 512
 
 
-def flash_body(lo_ref, hi_ref, q_ref, k_ref, v_ref, tok_ref, begin_ref, o_ref):
+def flash_body(lo_ref, hi_ref, in_lo_ref, in_hi_ref, q_ref, k_ref, v_ref, tok_ref, begin_ref, o_ref):
     qb = pl.program_id(1)
     ratio = q_ref.shape[1]
     q_tile = q_ref.shape[2]
@@ -138,9 +138,14 @@
             q, k_blk, (((1,), (1,)), ((), ())), preferred_element_type=jnp.float32
         )
         s = (s * score_scale).reshape(ratio, q_tile, K_TILE)
-        key_at = k0 + lax.broadcasted_iota(jnp.int32, (q_tile, K_TILE), 1)
-        allowed = (key_at >= begin) & (key_at <= tok)
-        s = jnp.where(allowed[None], s, -jnp.inf)
+        inside = (kb >= in_lo_ref[qb]) & (kb <= in_hi_ref[qb])
+
+        def masked(s_in):
+            key_at = k0 + lax.broadcasted_iota(jnp.int32, (q_tile, K_TILE), 1)
+            allowed = (key_at >= begin) & (key_at <= tok)
+            return jnp.where(allowed[None], s_in, -jnp.inf)
+
+        s = lax.cond(inside, lambda s_in: s_in, masked, s)
         m_new = jnp.maximum(m_old, jnp.max(s, axis=-1, keepdims=True))
         alpha = jnp.exp(m_old - m_new)
         p = jnp.exp(s - m_new)
@@ -169,25 +174,27 @@
     n_q = group_len // Q_TILE
     lo = jnp.min(q_begin.reshape(n_q, Q_TILE), axis=1) // K_TILE
     hi = jnp.max(q_index.reshape(n_q, Q_TILE), axis=1) // K_TILE
+    in_lo = -(-jnp.max(q_begin.reshape(n_q, Q_TILE), axis=1) // K_TILE)
+    in_hi = (jnp.min(q_index.reshape(n_q, Q_TILE), axis=1) + 1) // K_TILE - 1
     grid_spec = pltpu.PrefetchScalarGridSpec(
-        num_scalar_prefetch=2,
+        num_scalar_prefetch=4,
         grid=(kv_heads, n_q),
         in_specs=[
-            pl.BlockSpec((1, ratio, Q_TILE, head_dim), lambda g, qb, lo, hi: (g, 0, qb, 0)),
-            pl.BlockSpec((n_grp, 1, grp_len, head_dim), lambda g, qb, lo, hi: (0, g, 0, 0)),
+            pl.BlockSpec((1, ratio, Q_TILE, head_dim), lambda g, qb, lo, hi, il, ih: (g, 0, qb, 0)),
+            pl.BlockSpec((n_grp, 1, grp_len, head_dim), lambda g, qb, lo, hi, il, ih: (0, g, 0, 0)),
             pl.BlockSpec(
-                (n_grp, 1, grp_len, head_dim), lambda g, qb, lo, hi: (0, kv_heads + g, 0, 0)
+                (n_grp, 1, grp_len, head_dim), lambda g, qb, lo, hi, il, ih: (0, kv_heads + g, 0, 0)
             ),
-            pl.BlockSpec((Q_TILE, 1), lambda g, qb, lo, hi: (qb, 0)),
-            pl.BlockSpec((Q_TILE, 1), lambda g, qb, lo, hi: (qb, 0)),
+            pl.BlockSpec((Q_TILE, 1), lambda g, qb, lo, hi, il, ih: (qb, 0)),
+            pl.BlockSpec((Q_TILE, 1), lambda g, qb, lo, hi, il, ih: (qb, 0)),
         ],
-        out_specs=pl.BlockSpec((1, ratio, Q_TILE, head_dim), lambda g, qb, lo, hi: (g, 0, qb, 0)),
+        out_specs=pl.BlockSpec((1, ratio, Q_TILE, head_dim), lambda g, qb, lo, hi, il, ih: (g, 0, qb, 0)),
     )
     out = pl.pallas_call(
         flash_body,
         grid_spec=grid_spec,
         out_shape=jax.ShapeDtypeStruct(query_grouped.shape, jnp.bfloat16),
-    )(lo, hi, query_grouped, kv_all, kv_all, q_index[:, None], q_begin[:, None])
+    )(lo, hi, in_lo, in_hi, query_grouped, kv_all, kv_all, q_index[:, None], q_begin[:, None])
     return out
 
 

time: 191 us -> 193 us (1.010)
  the two profiles are of different devices: /device:TPU:24 before, /device:TPU:12 now
where the time goes in v2:
time: 193 us; the launch traced here: 192 us
  waiting for transfers between devices  61.1 us (32%)
  matrix products  37 us (19%)
  local copies, waits for them, and re-layouts  27.7 us (14%)
  Pallas kernels  26.5 us (14%)
  other arithmetic  20.5 us (11%)
  starting transfers between devices  18.4 us (10%)
    all_to_all x1, waiting for transfers between devices, body(): lax.all_to_all(jnp.broadcast_to(kv_local[None], (req_count,) + kv_local.s...  29.9 us
    pallas_call x1, Pallas kernels, flash_attention(): pl.pallas_call(flash_body, grid_spec=grid_spec, out_shape=jax.ShapeDtypeS...  26.5 us
    dot_general x1, matrix products, body(): jnp.einsum('esd,edf->esf', arrived, w_in, preferred_element_type=jnp.floa...  17.3 us
    ppermute x2, waiting for transfers between devices, scatter_sum_ep(): lax.ppermute(piece.astype(jnp.bfloat16), 'ep', chip_pairs(count, shift))  16.9 us
    dot_general x1, matrix products, body(): jnp.einsum('esr,esd->rd', combine.astype(jnp.bfloat16), result, preferred...  14.5 us
    all_to_all x2, starting transfers between devices, gather_rows(): got = lax.all_to_all(spread, axis_name, 0, 0, tiled=True)  8.54 us
    ppermute x2, waiting for transfers between devices, gather_ep(): side.append(lax.ppermute(x, 'ep', chip_pairs(count, shift)))  7.84 us
    all_to_all x1, starting transfers between devices, body(): lax.all_to_all(jnp.broadcast_to(kv_local[None], (req_count,) + kv_local.s...  5.88 us
  transfers between devices with their start and end apart: 11, of which 10 were waited for; matrix products, arithmetic and copies ran while one was open for 14% of the time, Pallas kernels for 0%

profile of v2, /device:TPU:12, one launch (start us, length us, event | category | flops | bytes accessed | tf_op | source)
XLA Modules:
  0.0 192.3 jit_solution(12328524681342620909)
XLA Ops:
  0.6 1.3 fusion.39
  3.1 1.6 collective-permute-start
  4.6 1.3 broadcast_in_dim.43
  5.9 5.1 %all-to-all-start = ((s32[32,1,128]{2,1,0:T(1,128)}), s32[32,1,128]{2,1,0:T(1,128)S(1)}, u32[]{:S(2)}, u32[]{:S(2)}) async-start(s32[32,1,128]{2,1,0:T(1,128)} %broadcast_in_dim.43), calls=%async_computation | async-start | bytes 32768 | tf_op jit(solution)/shard_map/all_to_all | solution.py:55
  12.1 1.9 collective-permute-done
  14.2 1.7 all-to-all-done
  16.7 1.6 multiply_cosine_fusion
  18.3 1.6 maximum_select_fusion
  19.9 2.1 %gather_fusion = bf16[2,2,128,1536]{3,2,1,0:T(8,128)(2,1)} fusion(bf16[2,2,128,1536]{3,2,0,1:T(8,128)(2,1)S(1)} %maximum_select_fusion, s32[1024]{0:T(1024)} %pad_clamp_fusion), kind=kCustom, calls=%fused_computation | custom fusion | bytes 3145736 | tf_op jit(solution)/shard_map/jit(_take)/gather | solution.py:89
  22.0 3.1 %fusion.23 = f32[512,640]{1,0:T(8,128)S(1)} fusion(bf16[512,1536]{1,0:T(8,128)(2,1)} %bitcast.137, bf16[1536,128]{1,0:T(8,128)(2,1)S(1)} %copy-done.14, bf16[1536,128]{1,0:T(8,128)(2,1)S(1)} %copy-done.15, bf16[1536,384]{1,0:T(8,128)(2,1)} %param.20), kind=kOutput, calls=%fused_computation.18 | convolution fusion | flops 1012531200 | bytes 4849664 | tf_op jit(solution)/shard_map/dot_general | solution.py:228
  26.6 1.6 broadcast_in_dim.49
  28.2 5.9 %all-to-all-start.1 = ((bf16[8,4,512,64]{2,3,1,0:T(8,128)(2,1)}), bf16[8,4,512,64]{2,3,1,0:T(8,128)(2,1)S(1)}, u32[]{:S(2)}, u32[]{:S(2)}) async-start(bf16[8,4,512,64]{2,3,1,0:T(8,128)(2,1)} %broadcast_in_dim.49), calls=%async_computation.1 | async-start | bytes 4194304 | tf_op jit(solution)/shard_map/all_to_all | solution.py:257
  37.2 2.1 %slice.79 = f32[512,384]{1,0:T(8,128)} slice(f32[512,640]{1,0:T(8,128)} %copy-done.6), slice={[0:512], [0:384]} | slice | bytes 1572864 | tf_op jit(solution)/shard_map/slice | solution.py:237
  39.3 2.3 %copy.93 = f32[512,384]{0,1:T(8,128)} copy(f32[512,384]{1,0:T(8,128)} %slice.79) | data formatting | bytes 1572864 | tf_op jit(solution)/shard_map/slice | solution.py:237
  41.6 1.9 subtract_convert_fusion
  43.5 2.1 %copy.94 = bf16[512,6,32]{2,0,1:T(8,128)(2,1)} copy(bf16[512,6,32]{0,2,1:T(8,128)(2,1)} %get-tuple-element.27) | data formatting | bytes 393216 | tf_op jit(solution)/shard_map/convert.8
  46.8 2.7 %maximum_bitcast_fusion.q_ref = bf16[2,3,512,64]{3,2,1,0:T(8,128)(2,1)} fusion(bf16[512,2,3,32]{3,0,2,1:T(8,128)(2,1)} %bitcast.134, bf16[512,2,3,32]{3,0,2,1:T(8,128)(2,1)} %bitcast.133), kind=kLoop, calls=%fused_computation.46 | loop fusion | flops 786432 | bytes 786432 | tf_op jit(solution)/shard_map/transpose | solution.py:250
  49.5 29.9 %all-to-all-done.1 = bf16[8,4,512,64]{2,3,1,0:T(8,128)(2,1)S(1)} async-done(((bf16[8,4,512,64]{2,3,1,0:T(8,128)(2,1)}), bf16[8,4,512,64]{2,3,1,0:T(8,128)(2,1)S(1)}, u32[]{:S(2)}, u32[]{:S(2)}) %all-to-all-start.1) | async-done | bytes 2097184 | tf_op jit(solution)/shard_map/all_to_all | solution.py:257
  79.3 3.2 %copy.98.k_ref.v_ref = bf16[8,4,512,64]{3,2,1,0:T(8,128)(2,1)} copy(bf16[8,4,512,64]{2,3,1,0:T(8,128)(2,1)S(1)} %all-to-all-done.1) | data formatting | bytes 4194304 | tf_op jit(solution)/shard_map/all_to_all | solution.py:257
  82.5 26.5 %shard_map.157 = bf16[2,3,512,64]{3,2,1,0:T(8,128)(2,1)} custom-call(s32[2]{0:T(128)} %get-tuple-element.40.lo_ref, s32[2]{0:T(128)} %get-tuple-element.39.hi_ref, s32[2]{0:T(128)} %get-tuple-element.42.in_lo_ref, s32[2]{0:T(128)} %get-tuple-element.41.in_hi_ref, bf16[2,3,512,64]{3,2,1,0:T(8,128)(2,1)} %maximum_bitcast_fusion.q_ref, ...), custom_call_target="tpu_custom_call" | custom-call | tf_op jit(solution)/shard_map/pallas_call | solution.py:193
  109.1 2.2 %fusion.17 = bf16[512,1536]{1,0:T(8,128)(2,1)S(1)} fusion(bf16[2,3,512,64]{3,2,1,0:T(8,128)(2,1)} %shard_map.157, bf16[2,3,64,1536]{3,2,1,0:T(8,128)(2,1)S(1)} %bitcast.126), kind=kOutput, calls=%fused_computation.16 | convolution fusion | flops 604766208 | bytes 3145728 | tf_op jit(solution)/shard_map/grtd,grdo->to/dot_general | solution.py:277
  112.6 2.2 %collective-permute-done.2 = bf16[2,128,1536]{2,1,0:T(8,128)(2,1)S(1)} collective-permute-done((bf16[2,128,1536]{2,1,0:T(8,128)(2,1)S(1)}, bf16[2,128,1536]{2,1,0:T(8,128)(2,1)S(1)}, u32[]{:S(2)}, u32[]{:S(2)}) %collective-permute-start.2) | collective-permute-done | bytes 786464 | tf_op jit(solution)/shard_map/ppermute | solution.py:105
  114.8 1.7 convert_add_fusion.1
  117.3 10.6 %collective-permute-done.3 = bf16[128,1536]{1,0:T(8,128)(2,1)S(1)} collective-permute-done((bf16[128,1536]{1,0:T(8,128)(2,1)S(1)}, bf16[128,1536]{1,0:T(8,128)(2,1)S(1)}, u32[]{:S(2)}, u32[]{:S(2)}) %collective-permute-start.3) | collective-permute-done | bytes 393248 | tf_op jit(solution)/shard_map/ppermute | solution.py:110
  130.3 3.5 %all-to-all-start.2 = ((f32[4,128,40]{1,2,0:T(8,128)}), f32[4,128,40]{1,2,0:T(8,128)S(1)}, u32[]{:S(2)}, u32[]{:S(2)}) async-start(f32[4,128,40]{1,2,0:T(8,128)} %broadcast_in_dim.53), calls=%async_computation.2 | async-start | bytes 163840 | tf_op jit(solution)/shard_map/all_to_all | solution.py:55
  133.9 5.9 %collective-permute-done.4 = bf16[128,1536]{1,0:T(8,128)(2,1)S(1)} collective-permute-done((bf16[128,1536]{1,0:T(8,128)(2,1)S(1)}, bf16[128,1536]{1,0:T(8,128)(2,1)S(1)}, u32[]{:S(2)}, u32[]{:S(2)}) %collective-permute-start.4) | collective-permute-done | bytes 393248 | tf_op jit(solution)/shard_map/ppermute | solution.py:84
  141.0 1.3 collective-permute-done.5
  142.6 2.0 %gather_fusion.1 = bf16[2,2,128,1536]{3,2,1,0:T(8,128)(2,1)} fusion(bf16[2,2,128,1536]{3,2,0,1:T(8,128)(2,1)S(1)} %maximum_select_fusion.1, s32[1024]{0:T(1024)} %pad_clamp_fusion), kind=kCustom, calls=%fused_computation.1 | custom fusion | bytes 3145736 | tf_op jit(solution)/shard_map/jit(_take)/gather | solution.py:89
  144.6 17.3 %fusion.4 = f32[10,192,1024]{2,1,0:T(8,128)} fusion(bf16[10,1536,1024]{2,1,0:T(8,128)(2,1)} %param.24, bf16[512,1536,1]{1,0,2:T(8,128)(2,1)} %bitcast.136, s32[10,512]{1,0:T(8,128)S(1)} %copy.106, pred[10,512]{1,0:T(8,128)(4,1)S(1)} %get-tuple-element.23), kind=kOutput, calls=%fused_computation.6 | convolution fusion | flops 9064611840 | bytes 40920064 | tf_op jit(solution)/shard_map/esd,edf->esf/dot_general | solution.py:307
  161.8 14.5 %fusion.18 = bf16[512,1536]{1,0:T(8,128)(2,1)S(1)} fusion(bf16[10,512,1536]{2,1,0:T(8,128)(2,1)} %param.25, f32[10,192,1024]{2,1,0:T(8,128)} %fusion.4, bf16[10,512]{1,0:T(8,128)(2,1)S(1)} %dynamic-slice_bitcast_fusion, s32[10,512]{1,0:T(8,128)S(1)} %copy.106, pred[10,512]{1,0:T(8,128)(4,1)S(1)} %get-tuple-element.23), kind=kOutput, calls=%fused_computation.17 | convolution fusion | flops 6052380672 | bytes 25201664 | tf_op jit(solution)/shard_map/esr,esd->rd/dot_general | solution.py:315
  181.1 2.9 %gather_fusion.2 = bf16[12,2,2,64,64]{4,3,2,1,0:T(8,128)(2,1)S(1)} fusion(bf16[8,2,2,8,64,64]{5,4,3,2,1,0:T(8,128)(2,1)} %bitcast.127, s32[12]{0:T(128)S(1)} %fusion.54), kind=kCustom, calls=%fused_computation.2 | custom fusion | bytes 786528 | tf_op jit(solution)/shard_map/gather | solution.py:271
  185.2 6.3 %collective-permute-done.7 = bf16[128,1536]{1,0:T(8,128)(2,1)S(1)} collective-permute-done((bf16[128,1536]{1,0:T(8,128)(2,1)S(1)}, bf16[128,1536]{1,0:T(8,128)(2,1)S(1)}, u32[]{:S(2)}, u32[]{:S(2)}) %collective-permute-start.7) | collective-permute-done | bytes 393248 | tf_op jit(solution)/shard_map/ppermute | solution.py:110
  (100 shorter events, 21.6 us)
Async XLA Ops:
  0.6 108.5 %copy-start = (bf16[384,1536]{1,0:T(8,128)(2,1)S(1)}, bf16[384,1536]{1,0:T(8,128)(2,1)}, u32[]{:S(2)}) copy-start(bf16[384,1536]{1,0:T(8,128)(2,1)} %param.23) | copy-start | bytes 3538948
  3.1 11.0 %collective-permute-start = (bf16[128,1536]{1,0:T(8,128)(2,1)S(1)}, bf16[128,1536]{1,0:T(8,128)(2,1)S(1)}, u32[]{:S(2)}, u32[]{:S(2)}) collective-permute-start(bf16[128,1536]{1,0:T(8,128)(2,1)S(1)} %fusion.41), channel_id=1, source_target_pairs={{0,2},{1,3},{2,0},{3,1},{4,6},{5,7},{6,4},{7,5},{8,10},{9,11},{10,... | collective-permute-start | bytes 1179656 | tf_op jit(solution)/shard_map/ppermute | solution.py:84
  5.9 10.0 %all-to-all-start = ((s32[32,1,128]{2,1,0:T(1,128)}), s32[32,1,128]{2,1,0:T(1,128)S(1)}, u32[]{:S(2)}, u32[]{:S(2)}) async-start(s32[32,1,128]{2,1,0:T(1,128)} %broadcast_in_dim.43), calls=%async_computation | async-start | bytes 32768 | tf_op jit(solution)/shard_map/all_to_all | solution.py:55
  14.2 4.2 %collective-permute-start.1 = (bf16[2,128,1536]{2,1,0:T(8,128)(2,1)S(1)}, bf16[2,128,1536]{2,1,0:T(8,128)(2,1)}, u32[]{:S(2)}, u32[]{:S(2)}) collective-permute-start(bf16[2,128,1536]{2,1,0:T(8,128)(2,1)S(1)} %get-tuple-element.32), channel_id=1, source_target_pairs={{0,1},{1,0},{2,3},{3,2},{4,5},{5,4},{6,7},{7,6},{8,9},{9,8},{10,11... | collective-permute-start | bytes 2359304 | tf_op jit(solution)/shard_map/ppermute | solution.py:86
  19.9 2.1 %copy-start.14 = (bf16[1536,128]{1,0:T(8,128)(2,1)S(1)}, bf16[1536,128]{1,0:T(8,128)(2,1)}, u32[]{:S(2)}) copy-start(bf16[1536,128]{1,0:T(8,128)(2,1)} %param.22) | copy-start | bytes 1179652
  19.9 2.1 %copy-start.15 = (bf16[1536,128]{1,0:T(8,128)(2,1)S(1)}, bf16[1536,128]{1,0:T(8,128)(2,1)}, u32[]{:S(2)}) copy-start(bf16[1536,128]{1,0:T(8,128)(2,1)} %param.21) | copy-start | bytes 1179652
  25.1 1.1 copy-start.6
  25.1 1.3 copy-start.8
  25.2 1.3 copy-start.9
  28.2 51.2 %all-to-all-start.1 = ((bf16[8,4,512,64]{2,3,1,0:T(8,128)(2,1)}), bf16[8,4,512,64]{2,3,1,0:T(8,128)(2,1)S(1)}, u32[]{:S(2)}, u32[]{:S(2)}) async-start(bf16[8,4,512,64]{2,3,1,0:T(8,128)(2,1)} %broadcast_in_dim.49), calls=%async_computation.1 | async-start | bytes 4194304 | tf_op jit(solution)/shard_map/all_to_all | solution.py:257
  111.3 1.2 copy-start.2
  112.5 2.4 %collective-permute-start.2 = (bf16[2,128,1536]{2,1,0:T(8,128)(2,1)S(1)}, bf16[2,128,1536]{2,1,0:T(8,128)(2,1)S(1)}, u32[]{:S(2)}, u32[]{:S(2)}) collective-permute-start(bf16[2,128,1536]{2,1,0:T(8,128)(2,1)S(1)} %select_bitcast_fusion.1), channel_id=1, source_target_pairs={{0,1},{1,0},{2,3},{3,2},{4,5},{5,4},{6,7},{7,6},{8,9},{9,8},{10,11... | collective-permute-start | bytes 2359304 | tf_op jit(solution)/shard_map/ppermute | solution.py:105
  112.6 15.2 %copy-start.3 = (bf16[128,1536]{1,0:T(8,128)(2,1)S(1)}, bf16[128,1536]{1,0:T(8,128)(2,1)}, u32[]{:S(2)}) copy-start(bf16[128,1536]{1,0:T(8,128)(2,1)} %param.14) | copy-start | bytes 1179652
  116.5 11.6 %copy-start.10 = (f32[1536]{0:T(1024)S(1)}, f32[1536]{0:T(1024)}, u32[]{:S(2)}) copy-start(f32[1536]{0:T(1024)} %param.19) | copy-start | bytes 18436
  116.6 11.2 %collective-permute-start.3 = (bf16[128,1536]{1,0:T(8,128)(2,1)S(1)}, bf16[128,1536]{1,0:T(8,128)(2,1)S(1)}, u32[]{:S(2)}, u32[]{:S(2)}) collective-permute-start(bf16[128,1536]{1,0:T(8,128)(2,1)S(1)} %fusion.43), channel_id=1, source_target_pairs={{0,2},{1,3},{2,0},{3,1},{4,6},{5,7},{6,4},{7,5},{8,10},{9,11},{10,... | collective-permute-start | bytes 1179656 | tf_op jit(solution)/shard_map/ppermute | solution.py:110
  128.1 1.6 copy-start.11
  128.1 1.6 copy-start.12
  129.1 10.8 %collective-permute-start.4 = (bf16[128,1536]{1,0:T(8,128)(2,1)S(1)}, bf16[128,1536]{1,0:T(8,128)(2,1)S(1)}, u32[]{:S(2)}, u32[]{:S(2)}) collective-permute-start(bf16[128,1536]{1,0:T(8,128)(2,1)S(1)} %get-tuple-element.25), channel_id=1, source_target_pairs={{0,2},{1,3},{2,0},{3,1},{4,6},{5,7},{6,4},{7,5},{8,10},{9,11},{10,... | collective-permute-start | bytes 1179656 | tf_op jit(solution)/shard_map/ppermute | solution.py:84
  130.3 9.9 %all-to-all-start.2 = ((f32[4,128,40]{1,2,0:T(8,128)}), f32[4,128,40]{1,2,0:T(8,128)S(1)}, u32[]{:S(2)}, u32[]{:S(2)}) async-start(f32[4,128,40]{1,2,0:T(8,128)} %broadcast_in_dim.53), calls=%async_computation.2 | async-start | bytes 163840 | tf_op jit(solution)/shard_map/all_to_all | solution.py:55
  139.9 2.4 %collective-permute-start.5 = (bf16[2,128,1536]{2,1,0:T(8,128)(2,1)S(1)}, bf16[2,128,1536]{2,1,0:T(8,128)(2,1)S(1)}, u32[]{:S(2)}, u32[]{:S(2)}) collective-permute-start(bf16[2,128,1536]{2,1,0:T(8,128)(2,1)S(1)} %get-tuple-element.30), channel_id=1, source_target_pairs={{0,1},{1,0},{2,3},{3,2},{4,5},{5,4},{6,7},{7,6},{8,9},{9,8},{10,11... | collective-permute-start | bytes 2359304 | tf_op jit(solution)/shard_map/ppermute | solution.py:86
  176.3 0.7 copy-start.13
  176.4 2.4 %collective-permute-start.6 = (bf16[2,128,1536]{2,1,0:T(8,128)(2,1)S(1)}, bf16[2,128,1536]{2,1,0:T(8,128)(2,1)S(1)}, u32[]{:S(2)}, u32[]{:S(2)}) collective-permute-start(bf16[2,128,1536]{2,1,0:T(8,128)(2,1)S(1)} %select_bitcast_fusion), channel_id=1, source_target_pairs={{0,1},{1,0},{2,3},{3,2},{4,5},{5,4},{6,7},{7,6},{8,9},{9,8},{10,11... | collective-permute-start | bytes 2359304 | tf_op jit(solution)/shard_map/ppermute | solution.py:105
  179.1 1.2 copy-start.4
  180.2 3.8 %copy-start.7 = (bf16[12,2,2,64,64]{4,3,2,1,0:T(8,128)(2,1)S(1)}, bf16[12,2,2,64,64]{4,3,2,1,0:T(8,128)(2,1)}, u32[]{:S(2)}) copy-start(bf16[12,2,2,64,64]{4,3,2,1,0:T(8,128)(2,1)} %param.26) | copy-start | bytes 1179652
  180.3 11.2 %collective-permute-start.7 = (bf16[128,1536]{1,0:T(8,128)(2,1)S(1)}, bf16[128,1536]{1,0:T(8,128)(2,1)S(1)}, u32[]{:S(2)}, u32[]{:S(2)}) collective-permute-start(bf16[128,1536]{1,0:T(8,128)(2,1)S(1)} %fusion.44), channel_id=1, source_target_pairs={{0,2},{1,3},{2,0},{3,1},{4,6},{5,7},{6,4},{7,5},{8,10},{9,11},{10,... | collective-permute-start | bytes 1179656 | tf_op jit(solution)/shard_map/ppermute | solution.py:110
  184.1 7.5 %copy-start.5 = (f32[2,128,1536]{2,1,0:T(8,128)S(1)}, f32[2,128,1536]{2,1,0:T(8,128)}, u32[]{:S(2)}) copy-start(f32[2,128,1536]{2,1,0:T(8,128)} %copy-done.4) | copy-start | bytes 4718596
  184.1 8.3 %copy-start.1 = (bf16[384,1536]{1,0:T(8,128)(2,1)S(1)}, bf16[384,1536]{1,0:T(8,128)(2,1)}, u32[]{:S(2)}) copy-start(bf16[384,1536]{1,0:T(8,128)(2,1)} %param.23) | copy-start | bytes 3538948
